TPU v7x, 128 devices: a whole 4x4x4 slice. The times are simulated.
128 devices in a mesh: wide: 16 (over z, y), col: 8 (over x, core).
Axes of the slice: x: 4, y: 4, z: 4, core: 2. Of those that a mesh axis runs over, the one named last changes fastest.
Arguments:
- z_root: float32 [512, 16384], P('col', 'wide'), may hold values from -6 to 6
- z_child: float32 [512, 2, 8192], P('col', None, 'wide'), may hold values from -6 to 6
- z_grand: float32 [512, 4, 4096], P('col', None, 'wide'), may hold values from -6 to 6
- inv_root: float32 [16384, 16384], P('wide', 'col'), as said below
- inv_child: float32 [2, 8192, 8192], P(None, 'wide', 'col'), as said below
- inv_grand: float32 [4, 4096, 4096], P(None, 'wide', 'col'), as said below
- panel_child: float32 [2, 4096, 8192], P(None, 'col', 'wide'), may hold values from -0.046875 to 0.046875
- panel_grand: float32 [4, 2048, 4096], P(None, 'col', 'wide'), may hold values from -0.0625 to 0.0625
- anc_child: int32 [2, 32], P(None, 'col'), may hold values from 0 to 127, as said below
- anc_grand: int32 [4, 16], P(None, 'col'), may hold values from 0 to 255, as said below
Outputs:
- x_root: float32 [512, 16384], P('wide', 'col')
- x_child: float32 [512, 2, 8192], P('wide', None, 'col')
- x_grand: float32 [512, 4, 4096], P('wide', None, 'col')
Inputs may be any that keep to these rules, and one draw needn't show every extreme that they name: inv_root is lower triangular with a positive diagonal (entries above the diagonal are zero). Each inv_child[k] is lower triangular with a positive diagonal. Each inv_grand[g] is lower triangular with a positive diagonal. `anc_child`: each row lists distinct blocks in rising order and always names block 0 and block 127. `anc_grand`: row g lists 2048 // 256 distinct root blocks in rising order, block 0 and block 127 among them, then as many distinct blocks of child g // 2 (numbered 16384 // 128 + (g // 2) * 64 onwards) in rising order, its first and its last among them.
All inputs are finite; a program needn't handle non-finite values.
Results may differ from a plain program's by a relative error of at most 0.000096.
Values sent between devices are 32-bit elements; how exact they have to be, the bound alone decides.
No kernel may reach another device: no remote copies, remote signals or barrier semaphores. Data moves between devices by JAX's collectives and lax.ppermute only.
A program may use at most 128 MiB of HBM per device.

v0:
```python
import jax
import jax.numpy as jnp
from jax import lax
from jax.sharding import PartitionSpec as P

BLK = 128
PRECISE = lax.Precision.HIGHEST


def pick_blocks(source_rows, blocks):
    leading = source_rows.shape[0]
    tiled = source_rows.reshape(leading, source_rows.shape[1] // BLK, BLK)
    selected = jnp.take(tiled, blocks.reshape(-1), axis=1)
    return selected.reshape(leading, blocks.shape[0], blocks.shape[1] * BLK)


def spread_rhs(local_part):
    return lax.all_gather(local_part, "col", axis=0, tiled=True)


def solve_terms(right_rows, inverse):
    return lax.psum_scatter(
        jnp.einsum(
            "ski,kij->skj",
            right_rows,
            inverse,
            precision=PRECISE,
            preferred_element_type=jnp.float32,
        ),
        "wide",
        scatter_dimension=0,
        tiled=True,
    )


def spread_solved(solved_local):
    gathered = lax.all_gather(solved_local, "col", axis=2, tiled=True)
    return gathered.reshape(gathered.shape[0], -1)


def fetch_ancestors(source_rows, blocks):
    return lax.all_gather(pick_blocks(source_rows, blocks), "wide", axis=0, tiled=True)


def finish_level(z_local, inverse, partial_value):
    summed = lax.psum(partial_value, "col")
    right_side = spread_rhs(z_local) - summed
    solved = solve_terms(right_side, inverse)
    return solved


def per_device(
    z_root,
    z_child,
    z_grand,
    inv_root,
    inv_child,
    inv_grand,
    panel_child,
    panel_grand,
    anc_child,
    anc_grand,
):
    root_right = spread_rhs(z_root[:, None, :])
    root_solved = solve_terms(root_right, inv_root[None])
    x_root = root_solved[:, 0, :]
    root_rows = spread_solved(root_solved)
    near_rows = fetch_ancestors(root_rows, anc_child)
    partial_value = jnp.einsum(
        "ska,kaj->skj",
        near_rows,
        panel_child,
        precision=PRECISE,
        preferred_element_type=jnp.float32,
    )
    x_child = finish_level(z_child, inv_child, partial_value)
    child_rows = spread_solved(x_child)
    solved_all = jnp.concatenate([root_rows, child_rows], axis=1)
    far_rows = fetch_ancestors(solved_all, anc_grand)
    partial_grand = jnp.einsum(
        "sga,gaj->sgj", far_rows, panel_grand, precision=PRECISE, preferred_element_type=jnp.float32
    )
    x_grand = finish_level(z_grand, inv_grand, partial_grand)
    return (x_root, x_child, x_grand)


def solution(mesh):
    in_specs = (
        P("col", "wide"),
        P("col", None, "wide"),
        P("col", None, "wide"),
        P("wide", "col"),
        P(None, "wide", "col"),
        P(None, "wide", "col"),
        P(None, "col", "wide"),
        P(None, "col", "wide"),
        P(None, "col"),
        P(None, "col"),
    )
    out_specs = (P("wide", "col"), P("wide", None, "col"), P("wide", None, "col"))
    return jax.shard_map(
        per_device, mesh=mesh, in_specs=in_specs, out_specs=out_specs, check_vma=False
    )
```

profile of v0, /device:TPU:0, one launch (start us, length us, event | category | flops | bytes accessed | tf_op | source)
XLA Modules:
  0.0 726.2 jit_solution(2255232434404925078)
XLA Ops:
  7.2 0.7 all-gather.21.cloned.1.call-update
  8.0 29.4 %all-gather.21.cloned.1.call-done = f32[512,1024]{1,0:T(8,128)} async-done(((f32[64,1024]{1,0:T(8,128)}), f32[512,1024]{1,0:T(8,128)}) %all-gather.21.cloned.1.call-update) | async-done | bytes 2097168 | tf_op jit(solution)/shard_map/all_gather | solution.py:18
  37.4 30.4 %convolution_bitcast_fusion = f32[512,1,2048]{0,2,1:T(8,128)} fusion(f32[1024,2048]{1,0:T(8,128)} %param.13, f32[512,1024]{1,0:T(8,128)} %all-gather.21.cloned.1.call-done), kind=kOutput, calls=%fused_computation.3 | convolution fusion | flops 12884901888 | bytes 14680064 | tf_op jit(solution)/shard_map/ski,kij->skj/dot_general | solution.py:23
  67.8 11.0 %copy.75 = f32[512,1,2048]{2,1,0:T(1,128)} copy(f32[512,1,2048]{0,2,1:T(8,128)} %convolution_bitcast_fusion) | data formatting | bytes 8388608 | tf_op jit(solution)/shard_map/ski,kij->skj/transpose | solution.py:23
  78.8 0.0 all-gather.11.cloned.1.call-start
  78.9 0.6 copy-done.8
  79.5 0.6 dynamic-slice
  80.7 102.2 %all-reduce.9.cloned.1.call-done = f32[512,1,2048]{2,1,0:T(1,128)} async-done(((f32[512,1,2048]{2,1,0:T(1,128)}), f32[512,1,2048]{2,1,0:T(1,128)}) %all-reduce.9.cloned.1.call-update) | async-done | bytes 4194320
  183.0 1.7 constant_dynamic-slice_fusion
  184.7 0.1 reshape.104
  184.8 0.1 broadcast_bitcast_fusion.1
  184.9 25.1 %all-gather.11.cloned.1.call-done = f32[32,1,16384]{2,1,0:T(1,128)} async-done(((f32[32,1,2048]{2,1,0:T(1,128)}), f32[32,1,16384]{2,1,0:T(1,128)}) %all-gather.11.cloned.1.call-update) | async-done | bytes 2097168 | tf_op jit(solution)/shard_map/all_gather | solution.py:37
  210.0 4.2 copy.77
  214.3 2.1 gather_fusion
  216.4 0.1 copy.78
  216.5 0.1 gather.13
  216.6 0.7 copy_select_fusion.1
  217.3 0.8 copy.76
  218.1 0.0 all-reduce.5.cloned.1.call-start
  218.2 44.9 %all-gather.13.cloned.1.call-done = f32[512,2,512]{2,0,1:T(8,128)} async-done(((f32[32,2,512]{2,0,1:T(8,128)}), f32[512,2,512]{2,0,1:T(8,128)}) %all-gather.13.cloned.1.call-update) | async-done | bytes 2097168 | tf_op jit(solution)/shard_map/all_gather | solution.py:42
  263.0 7.0 convolution_bitcast_fusion.4
  270.1 19.4 %all-gather.9.cloned.1.call-done = f32[512,2,512]{2,0,1:T(8,128)} async-done(((f32[64,2,512]{2,0,1:T(8,128)}), f32[512,2,512]{2,0,1:T(8,128)}) %all-gather.9.cloned.1.call-update) | async-done | bytes 2097168 | tf_op jit(solution)/shard_map/all_gather | solution.py:18
  289.6 68.2 %all-reduce.5.cloned.1.call-done = f32[512,2,512]{2,0,1:T(8,128)} async-done(((f32[512,2,512]{2,0,1:T(8,128)}), f32[512,2,512]{2,0,1:T(8,128)}) %all-reduce.5.cloned.1.call-update) | async-done | bytes 2097168 | tf_op jit(solution)/shard_map/psum | solution.py:46
  357.8 12.2 %convolution_bitcast_fusion.2 = f32[512,2,1024]{2,0,1:T(8,128)} fusion(f32[2,512,1024]{2,1,0:T(8,128)} %param.14, f32[512,2,512]{2,0,1:T(8,128)} %all-gather.9.cloned.1.call-done, f32[512,2,512]{2,0,1:T(8,128)} %all-reduce.5.cloned.1.call-done), kind=kOutput, calls=%fused_computation.5 | convolution fusion | flops 6442975232 | bytes 12582912 | tf_op jit(solution)/shard_map/ski,kij->skj/dot_general | solution.py:23
  370.1 77.5 %reduce-scatter.3.cloned.1.call-done = f32[32,2,1024]{2,0,1:T(8,128)} async-done(((f32[512,2,1024]{2,0,1:T(8,128)}), f32[32,2,1024]{2,0,1:T(8,128)}) %reduce-scatter.3.cloned.1.call-update) | async-done | bytes 262160 | tf_op jit(solution)/shard_map/reduce_scatter | solution.py:22
  447.6 0.1 copy.84
  447.7 0.1 reshape.105
  447.9 0.1 broadcast_bitcast_fusion
  447.9 25.8 %all-gather.17.cloned.1.call-done = f32[32,2,8192]{2,0,1:T(8,128)} async-done(((f32[32,2,1024]{2,0,1:T(8,128)}), f32[32,2,8192]{2,0,1:T(8,128)}) %all-gather.17.cloned.1.call-update) | async-done | bytes 2097168 | tf_op jit(solution)/shard_map/all_gather | solution.py:37
  473.7 4.6 copy.81
  478.3 4.0 concatenate.6
  482.3 3.0 copy.83
  485.3 2.4 pad_maximum_fusion
  487.7 2.8 gather_fusion.1
  490.5 0.1 copy.85
  490.6 0.1 gather.15
  490.7 0.7 copy_select_fusion
  491.4 1.7 copy.80
  493.2 43.9 %all-gather.19.cloned.1.call-done = f32[512,4,256]{2,0,1:T(8,128)} async-done(((f32[32,4,256]{2,0,1:T(8,128)}), f32[512,4,256]{2,0,1:T(8,128)}) %all-gather.19.cloned.1.call-update) | async-done | bytes 2097168 | tf_op jit(solution)/shard_map/all_gather | solution.py:42
  537.1 4.9 convolution_bitcast_fusion.3
  542.1 21.7 %all-gather.15.cloned.1.call-done = f32[512,4,256]{2,0,1:T(8,128)} async-done(((f32[64,4,256]{2,0,1:T(8,128)}), f32[512,4,256]{2,0,1:T(8,128)}) %all-gather.15.cloned.1.call-update) | async-done | bytes 2097168 | tf_op jit(solution)/shard_map/all_gather | solution.py:18
  563.8 68.5 %all-reduce.7.cloned.1.call-done = f32[512,4,256]{2,0,1:T(8,128)} async-done(((f32[512,4,256]{2,0,1:T(8,128)}), f32[512,4,256]{2,0,1:T(8,128)}) %all-reduce.7.cloned.1.call-update) | async-done | bytes 2097168 | tf_op jit(solution)/shard_map/psum | solution.py:46
  632.3 7.8 %convolution_bitcast_fusion.1 = f32[512,4,512]{2,0,1:T(8,128)} fusion(f32[4,256,512]{2,1,0:T(8,128)S(1)} %copy-done, f32[512,4,256]{2,0,1:T(8,128)} %all-gather.15.cloned.1.call-done, f32[512,4,256]{2,0,1:T(8,128)} %all-reduce.7.cloned.1.call-done), kind=kOutput, calls=%fused_computation.4 | convolution fusion | flops 3221749760 | bytes 10485760 | tf_op jit(solution)/shard_map/ski,kij->skj/dot_general | solution.py:23
  640.0 0.9 copy-done.2
  641.0 0.8 copy.95
  641.8 0.9 copy.87
  642.7 74.9 %reduce-scatter.5.cloned.1.call-done = f32[32,4,512]{2,0,1:T(8,128)} async-done(((f32[512,4,512]{2,0,1:T(8,128)}), f32[32,4,512]{2,0,1:T(8,128)}) %reduce-scatter.5.cloned.1.call-update) | async-done | bytes 262160 | tf_op jit(solution)/shard_map/reduce_scatter | solution.py:22
  717.6 1.8 copy.88
  (44 shorter events, 0.7 us)
Async XLA Ops:
  7.2 625.1 %copy-start = (f32[4,256,512]{2,1,0:T(8,128)S(1)}, f32[4,256,512]{2,1,0:T(8,128)}, u32[]{:S(2)}) copy-start(f32[4,256,512]{2,1,0:T(8,128)} %param.15) | copy-start | bytes 6291460
  7.2 30.2 %all-gather.21.cloned.1.call-start = ((), (), s32[]{:S(2)}) async-start(), calls=%async_computation.12 | async-start | bytes 2359296 | tf_op jit(solution)/shard_map/all_gather | solution.py:18
  7.9 175.0 %all-reduce.9.cloned.1.call-start = ((), (), s32[]{:S(2)}) async-start(), calls=%async_computation.13 | async-start | bytes 8388608
  78.8 0.7 copy-start.8
  78.8 105.9 %copy-start.7 = (s32[2,4]{1,0:T(2,128)S(1)}, s32[2,4]{1,0:T(2,128)}, u32[]{:S(2)}) copy-start(s32[2,4]{1,0:T(2,128)} %param.18) | copy-start | bytes 100
  78.8 131.2 %all-gather.11.cloned.1.call-start = ((), (), s32[]{:S(2)}) async-start(), calls=%async_computation.3 | async-start | bytes 2359296 | tf_op jit(solution)/shard_map/all_gather | solution.py:37
  184.7 78.4 %all-gather.13.cloned.1.call-start = ((), (), s32[]{:S(2)}) async-start(), calls=%async_computation.4 | async-start | bytes 2228224 | tf_op jit(solution)/shard_map/all_gather | solution.py:42
  210.0 7.3 %copy-start.5 = (f32[64,2,512]{2,1,0:T(2,128)S(1)}, f32[64,2,512]{2,1,0:T(2,128)}, u32[]{:S(2)}) copy-start(f32[64,2,512]{2,1,0:T(2,128)} %param.11) | copy-start | bytes 786436
  217.3 72.3 %all-gather.9.cloned.1.call-start = ((), (), s32[]{:S(2)}) async-start(), calls=%async_computation.2 | async-start | bytes 2359296 | tf_op jit(solution)/shard_map/all_gather | solution.py:18
  218.1 139.7 %all-reduce.5.cloned.1.call-start = ((), (), s32[]{:S(2)}) async-start(), calls=%async_computation.5 | async-start | bytes 4194304 | tf_op jit(solution)/shard_map/psum | solution.py:46
  270.1 177.5 %reduce-scatter.3.cloned.1.call-start = ((), (), s32[]{:S(2)}) async-start(), calls=%async_computation.6 | async-start | bytes 4456448 | tf_op jit(solution)/shard_map/reduce_scatter | solution.py:22
  370.0 77.7 %copy-start.6 = (s32[4,2]{0,1:T(2,128)S(1)}, s32[4,2]{0,1:T(2,128)}, u32[]{:S(2)}) copy-start(s32[4,2]{0,1:T(2,128)} %param.19) | copy-start | bytes 100
  370.0 103.7 %all-gather.17.cloned.1.call-start = ((), (), s32[]{:S(2)}) async-start(), calls=%async_computation.8 | async-start | bytes 2359296 | tf_op jit(solution)/shard_map/all_gather | solution.py:37
  447.6 89.6 %all-gather.19.cloned.1.call-start = ((), (), s32[]{:S(2)}) async-start(), calls=%async_computation.9 | async-start | bytes 2228224 | tf_op jit(solution)/shard_map/all_gather | solution.py:42
  482.3 3.0 copy-start.1
  487.7 49.5 %copy-start.3 = (f32[4,256,256]{2,1,0:T(8,128)S(1)}, f32[4,256,256]{2,1,0:T(8,128)}, u32[]{:S(2)}) copy-start(f32[4,256,256]{2,1,0:T(8,128)} %param.17) | copy-start | bytes 3145732
  491.4 72.4 %all-gather.15.cloned.1.call-start = ((), (), s32[]{:S(2)}) async-start(), calls=%async_computation.7 | async-start | bytes 2359296 | tf_op jit(solution)/shard_map/all_gather | solution.py:18
  493.2 139.1 %all-reduce.7.cloned.1.call-start = ((), (), s32[]{:S(2)}) async-start(), calls=%async_computation.10 | async-start | bytes 4194304 | tf_op jit(solution)/shard_map/psum | solution.py:46
  542.0 175.5 %reduce-scatter.5.cloned.1.call-start = ((), (), s32[]{:S(2)}) async-start(), calls=%async_computation.11 | async-start | bytes 4456448 | tf_op jit(solution)/shard_map/reduce_scatter | solution.py:22
  640.0 0.9 copy-start.2
  640.0 1.7 copy-start.4
Sparse Core Ops, SparseCore 0:
  9.7 27.5 all-gather.20
  79.0 103.9 all-reduce.8
  185.2 24.7 all-gather.10
  217.4 45.5 all-gather.12
  265.2 24.3 all-gather.8
  291.8 65.9 all-reduce.4
  370.1 77.3 reduce-scatter.2
  449.4 24.3 all-gather.16
  491.5 45.5 all-gather.18
  539.4 24.3 all-gather.14
  566.3 65.9 all-reduce.6
  640.2 77.3 reduce-scatter.4
where the time goes:
time: 727 us; the launch traced here: 726 us
  waiting for transfers between devices  602 us (83%)
  matrix products  62.3 us (9%)
  local copies, waits for them, and re-layouts  42.2 us (6%)
  between operations  15 us (2%)
    reduce_scatter x2, waiting for transfers between devices, solve_terms(): lax.psum_scatter(jnp.einsum('ski,kij->skj', right_rows, inverse, precisio...  152 us
    psum x2, waiting for transfers between devices, finish_level(): summed = lax.psum(partial_value, 'col')  137 us
    unnamed x13, waiting for transfers between devices  103 us
    all_gather x2, waiting for transfers between devices, fetch_ancestors(): lax.all_gather(pick_blocks(source_rows, blocks), 'wide', axis=0, tiled=True)  88.8 us
    all_gather x3, waiting for transfers between devices, spread_rhs(): return lax.all_gather(local_part, 'col', axis=0, tiled=True)  70.5 us
    all_gather x2, waiting for transfers between devices, spread_solved(): gathered = lax.all_gather(solved_local, 'col', axis=2, tiled=True)  50.9 us
    dot_general x3, matrix products, solve_terms(): jnp.einsum('ski,kij->skj', right_rows, inverse, precision=PRECISE, prefer...  50.4 us
  transfers between devices with their start and end apart: 12, of which 12 were waited for; matrix products, arithmetic and copies ran while one was open for 2% of the time, Pallas kernels for 0%

commit v1 on v0

--- a/solution.py
+++ b/solution.py
@@ -43,7 +43,8 @@
 
 
 def finish_level(z_local, inverse, partial_value):
-    summed = lax.psum(partial_value, "col")
+    parts = lax.all_gather(partial_value, "col")
+    summed = jnp.sum(parts, axis=0)
     right_side = spread_rhs(z_local) - summed
     solved = solve_terms(right_side, inverse)
     return solved

time: 727 us -> 775 us (1.066)
  waiting for transfers between devices: 602 us -> 634 us
  other arithmetic: 3.81 us -> 21.7 us
    all_gather x0 -> x2, waiting for transfers between devices: none -> 167 us  [finish_level(): parts = lax.all_gather(partial_value, 'col')]
    psum x2 -> x0, waiting for transfers between devices: 137 us -> none  [finish_level(): summed = lax.psum(partial_value, 'col')]
    reduce_sum x0 -> x2, other arithmetic: none -> 17.9 us  [finish_level(): summed = jnp.sum(parts, axis=0)]
  transfers between devices with their start and end apart: 12 -> 12, of which waited for: 12 -> 12; matrix products, arithmetic and copies ran while one was open for 2% -> 3% of each run, Pallas kernels for 0% -> 0%
where the time goes in v1:
time: 775 us; the launch traced here: 774 us
  waiting for transfers between devices  634 us (82%)
  matrix products  63.3 us (8%)
  local copies, waits for them, and re-layouts  39.6 us (5%)
  other arithmetic  21.7 us (3%)
  between operations  15 us (2%)
    all_gather x2, waiting for transfers between devices, finish_level(): parts = lax.all_gather(partial_value, 'col')  167 us
    reduce_scatter x2, waiting for transfers between devices, solve_terms(): lax.psum_scatter(jnp.einsum('ski,kij->skj', right_rows, inverse, precisio...  154 us
    unnamed x13, waiting for transfers between devices  104 us
    all_gather x2, waiting for transfers between devices, fetch_ancestors(): lax.all_gather(pick_blocks(source_rows, blocks), 'wide', axis=0, tiled=True)  91.4 us
    all_gather x3, waiting for transfers between devices, spread_rhs(): return lax.all_gather(local_part, 'col', axis=0, tiled=True)  66.5 us
    dot_general x3, matrix products, solve_terms(): jnp.einsum('ski,kij->skj', right_rows, inverse, precision=PRECISE, prefer...  51.3 us
    all_gather x2, waiting for transfers between devices, spread_solved(): gathered = lax.all_gather(solved_local, 'col', axis=2, tiled=True)  50.7 us
    reduce_sum x2, other arithmetic, finish_level(): summed = jnp.sum(parts, axis=0)  17.9 us
  transfers between devices with their start and end apart: 12, of which 12 were waited for; matrix products, arithmetic and copies ran while one was open for 3% of the time, Pallas kernels for 0%

profile of v1, /device:TPU:0, one launch (start us, length us, event | category | flops | bytes accessed | tf_op | source)
XLA Modules:
  0.0 774.3 jit_solution(989977373798437823)
XLA Ops:
  7.2 0.7 all-gather.25.cloned.1.call-update
  8.0 29.4 %all-gather.25.cloned.1.call-done = f32[512,1024]{1,0:T(8,128)} async-done(((f32[64,1024]{1,0:T(8,128)}), f32[512,1024]{1,0:T(8,128)}) %all-gather.25.cloned.1.call-update) | async-done | bytes 2097168 | tf_op jit(solution)/shard_map/all_gather | solution.py:18
  37.4 30.4 %convolution_bitcast_fusion = f32[512,1,2048]{0,2,1:T(8,128)} fusion(f32[1024,2048]{1,0:T(8,128)} %param.13, f32[512,1024]{1,0:T(8,128)} %all-gather.25.cloned.1.call-done), kind=kOutput, calls=%fused_computation.3 | convolution fusion | flops 12884901888 | bytes 14680064 | tf_op jit(solution)/shard_map/ski,kij->skj/dot_general | solution.py:23
  67.8 11.0 %copy.56 = f32[512,1,2048]{2,1,0:T(1,128)} copy(f32[512,1,2048]{0,2,1:T(8,128)} %convolution_bitcast_fusion) | data formatting | bytes 8388608 | tf_op jit(solution)/shard_map/ski,kij->skj/transpose | solution.py:23
  78.9 0.6 copy-done.7
  79.5 0.6 dynamic-slice
  80.7 102.2 %all-reduce.3.cloned.1.call-done = f32[512,1,2048]{2,1,0:T(1,128)} async-done(((f32[512,1,2048]{2,1,0:T(1,128)}), f32[512,1,2048]{2,1,0:T(1,128)}) %all-reduce.3.cloned.1.call-update) | async-done | bytes 4194320
  183.0 1.7 constant_dynamic-slice_fusion
  184.7 0.1 reshape.104
  184.8 0.1 broadcast_bitcast_fusion.1
  184.9 25.1 %all-gather.15.cloned.1.call-done = f32[32,1,16384]{2,1,0:T(1,128)} async-done(((f32[32,1,2048]{2,1,0:T(1,128)}), f32[32,1,16384]{2,1,0:T(1,128)}) %all-gather.15.cloned.1.call-update) | async-done | bytes 2097168 | tf_op jit(solution)/shard_map/all_gather | solution.py:37
  210.1 4.1 copy.57
  214.2 2.1 gather_fusion
  216.4 0.1 copy.58
  216.4 0.1 gather.13
  216.5 0.7 copy_select_fusion.1
  217.3 45.7 %all-gather.17.cloned.1.call-done = f32[512,2,512]{2,0,1:T(8,128)} async-done(((f32[32,2,512]{2,0,1:T(8,128)}), f32[512,2,512]{2,0,1:T(8,128)}) %all-gather.17.cloned.1.call-update) | async-done | bytes 2097168 | tf_op jit(solution)/shard_map/all_gather | solution.py:42
  263.0 7.1 convolution_bitcast_fusion.4
  270.2 0.5 all-gather.13.cloned.1.call-update
  270.7 83.6 %all-gather.27.cloned.1.call-done = f32[4096,2,512]{2,0,1:T(8,128)} async-done(((f32[512,2,512]{2,0,1:T(8,128)}), f32[4096,2,512]{2,0,1:T(8,128)}) %all-gather.27.cloned.1.call-update) | async-done | bytes 16777232 | tf_op jit(solution)/shard_map/all_gather | solution.py:46
  354.4 9.4 %reduce_sum.18 = f32[512,2,512]{2,0,1:T(8,128)} reduce(f32[8,512,2,512]{3,1,0,2:T(8,128)} %bitcast.41, f32[]{:T(128)} %constant.29.clone.1), dimensions={0}, to_apply=%region_1.2 | reduce | flops 3670016 | bytes 18874372 | tf_op jit(solution)/shard_map/reduce_sum | solution.py:47
  363.8 17.9 %all-gather.13.cloned.1.call-done = f32[512,2,512]{2,1,0:T(2,128)} async-done(((f32[64,2,512]{2,1,0:T(2,128)}), f32[512,2,512]{2,1,0:T(2,128)}) %all-gather.13.cloned.1.call-update) | async-done | bytes 2097168 | tf_op jit(solution)/shard_map/all_gather | solution.py:18
  381.8 12.4 %convolution_bitcast_fusion.2 = f32[512,2,1024]{2,0,1:T(8,128)} fusion(f32[2,512,1024]{2,1,0:T(8,128)} %param.14, f32[512,2,512]{2,0,1:T(8,128)} %reduce_sum.18, f32[512,2,512]{2,1,0:T(2,128)} %all-gather.13.cloned.1.call-done), kind=kOutput, calls=%fused_computation.5 | convolution fusion | flops 6442975232 | bytes 12582912 | tf_op jit(solution)/shard_map/ski,kij->skj/dot_general | solution.py:23
  394.3 78.2 %reduce-scatter.3.cloned.1.call-done = f32[32,2,1024]{2,0,1:T(8,128)} async-done(((f32[512,2,1024]{2,0,1:T(8,128)}), f32[32,2,1024]{2,0,1:T(8,128)}) %reduce-scatter.3.cloned.1.call-update) | async-done | bytes 262160 | tf_op jit(solution)/shard_map/reduce_scatter | solution.py:22
  472.5 0.3 all-gather.23.cloned.1.call-start
  472.8 0.1 copy.64
  472.9 0.1 reshape.105
  473.0 0.1 broadcast_bitcast_fusion
  473.0 25.6 %all-gather.21.cloned.1.call-done = f32[32,2,8192]{2,0,1:T(8,128)} async-done(((f32[32,2,1024]{2,0,1:T(8,128)}), f32[32,2,8192]{2,0,1:T(8,128)}) %all-gather.21.cloned.1.call-update) | async-done | bytes 2097168 | tf_op jit(solution)/shard_map/all_gather | solution.py:37
  498.6 4.5 copy.61
  503.2 4.0 concatenate.6
  507.2 3.0 copy.63
  510.2 2.4 pad_maximum_fusion
  512.6 2.7 gather_fusion.1
  515.3 0.1 copy.65
  515.5 0.7 copy_select_fusion
  516.2 45.7 %all-gather.23.cloned.1.call-done = f32[512,4,256]{2,0,1:T(8,128)} async-done(((f32[32,4,256]{2,0,1:T(8,128)}), f32[512,4,256]{2,0,1:T(8,128)}) %all-gather.23.cloned.1.call-update) | async-done | bytes 2097168 | tf_op jit(solution)/shard_map/all_gather | solution.py:42
  562.0 4.9 convolution_bitcast_fusion.3
  566.9 0.7 all-gather.19.cloned.1.call-update
  567.6 83.5 %all-gather.29.cloned.1.call-done = f32[4096,4,256]{2,0,1:T(8,128)} async-done(((f32[512,4,256]{2,0,1:T(8,128)}), f32[4096,4,256]{2,0,1:T(8,128)}) %all-gather.29.cloned.1.call-update) | async-done | bytes 16777232 | tf_op jit(solution)/shard_map/all_gather | solution.py:46
  651.1 8.4 %reduce_sum.19 = f32[512,4,256]{2,0,1:T(8,128)} reduce(f32[8,512,4,256]{3,1,0,2:T(8,128)} %bitcast.40, f32[]{:T(128)} %constant.29.clone.1), dimensions={0}, to_apply=%region_3.4 | reduce | flops 3670016 | bytes 18874372 | tf_op jit(solution)/shard_map/reduce_sum | solution.py:47
  659.6 19.2 %all-gather.19.cloned.1.call-done = f32[512,4,256]{2,1,0:T(4,128)} async-done(((f32[64,4,256]{2,1,0:T(4,128)}), f32[512,4,256]{2,1,0:T(4,128)}) %all-gather.19.cloned.1.call-update) | async-done | bytes 2097168 | tf_op jit(solution)/shard_map/all_gather | solution.py:18
  678.8 8.5 %convolution_bitcast_fusion.1 = f32[512,4,512]{2,0,1:T(8,128)} fusion(f32[4,256,512]{2,1,0:T(8,128)S(1)} %copy-done, f32[512,4,256]{2,0,1:T(8,128)} %reduce_sum.19, f32[512,4,256]{2,1,0:T(4,128)} %all-gather.19.cloned.1.call-done), kind=kOutput, calls=%fused_computation.4 | convolution fusion | flops 3221749760 | bytes 10485760 | tf_op jit(solution)/shard_map/ski,kij->skj/dot_general | solution.py:23
  687.3 0.9 copy-done.2
  688.2 0.8 copy.80
  689.0 0.9 copy.68
  689.9 75.7 %reduce-scatter.5.cloned.1.call-done = f32[32,4,512]{2,0,1:T(8,128)} async-done(((f32[512,4,512]{2,0,1:T(8,128)}), f32[32,4,512]{2,0,1:T(8,128)}) %reduce-scatter.5.cloned.1.call-update) | async-done | bytes 262160 | tf_op jit(solution)/shard_map/reduce_scatter | solution.py:22
  765.6 1.8 copy.69
  (42 shorter events, 0.7 us)
Async XLA Ops:
  7.2 671.6 %copy-start = (f32[4,256,512]{2,1,0:T(8,128)S(1)}, f32[4,256,512]{2,1,0:T(8,128)}, u32[]{:S(2)}) copy-start(f32[4,256,512]{2,1,0:T(8,128)} %param.15) | copy-start | bytes 6291460
  7.2 30.2 %all-gather.25.cloned.1.call-start = ((), (), s32[]{:S(2)}) async-start(), calls=%async_computation.10 | async-start | bytes 2359296 | tf_op jit(solution)/shard_map/all_gather | solution.py:18
  7.9 175.1 %all-reduce.3.cloned.1.call-start = ((), (), s32[]{:S(2)}) async-start(), calls=%async_computation.13 | async-start | bytes 8388608
  78.8 0.7 copy-start.7
  78.8 105.9 %copy-start.6 = (s32[2,4]{1,0:T(2,128)S(1)}, s32[2,4]{1,0:T(2,128)}, u32[]{:S(2)}) copy-start(s32[2,4]{1,0:T(2,128)} %param.18) | copy-start | bytes 100
  78.9 131.2 %all-gather.15.cloned.1.call-start = ((), (), s32[]{:S(2)}) async-start(), calls=%async_computation.3 | async-start | bytes 2359296 | tf_op jit(solution)/shard_map/all_gather | solution.py:37
  184.7 78.3 %all-gather.17.cloned.1.call-start = ((), (), s32[]{:S(2)}) async-start(), calls=%async_computation.4 | async-start | bytes 2228224 | tf_op jit(solution)/shard_map/all_gather | solution.py:42
  217.2 137.2 %all-gather.27.cloned.1.call-start = ((), (), s32[]{:S(2)}) async-start(), calls=%async_computation.11 | async-start | bytes 18874368 | tf_op jit(solution)/shard_map/all_gather | solution.py:46
  270.1 111.7 %all-gather.13.cloned.1.call-start = ((), (), s32[]{:S(2)}) async-start(), calls=%async_computation.2 | async-start | bytes 2359296 | tf_op jit(solution)/shard_map/all_gather | solution.py:18
  270.7 201.8 %reduce-scatter.3.cloned.1.call-start = ((), (), s32[]{:S(2)}) async-start(), calls=%async_computation.5 | async-start | bytes 4456448 | tf_op jit(solution)/shard_map/reduce_scatter | solution.py:22
  394.2 78.6 %copy-start.5 = (s32[4,2]{0,1:T(2,128)S(1)}, s32[4,2]{0,1:T(2,128)}, u32[]{:S(2)}) copy-start(s32[4,2]{0,1:T(2,128)} %param.19) | copy-start | bytes 100
  394.2 104.4 %all-gather.21.cloned.1.call-start = ((), (), s32[]{:S(2)}) async-start(), calls=%async_computation.7 | async-start | bytes 2359296 | tf_op jit(solution)/shard_map/all_gather | solution.py:37
  472.5 89.5 %all-gather.23.cloned.1.call-start = ((), (), s32[]{:S(2)}) async-start(), calls=%async_computation.8 | async-start | bytes 2228224 | tf_op jit(solution)/shard_map/all_gather | solution.py:42
  507.2 3.0 copy-start.1
  510.2 51.8 %copy-start.3 = (f32[4,256,256]{2,1,0:T(8,128)S(1)}, f32[4,256,256]{2,1,0:T(8,128)}, u32[]{:S(2)}) copy-start(f32[4,256,256]{2,1,0:T(8,128)} %param.17) | copy-start | bytes 3145732
  516.2 134.9 %all-gather.29.cloned.1.call-start = ((), (), s32[]{:S(2)}) async-start(), calls=%async_computation.12 | async-start | bytes 18874368 | tf_op jit(solution)/shard_map/all_gather | solution.py:46
  566.9 111.9 %all-gather.19.cloned.1.call-start = ((), (), s32[]{:S(2)}) async-start(), calls=%async_computation.6 | async-start | bytes 2359296 | tf_op jit(solution)/shard_map/all_gather | solution.py:18
  567.6 198.0 %reduce-scatter.5.cloned.1.call-start = ((), (), s32[]{:S(2)}) async-start(), calls=%async_computation.9 | async-start | bytes 4456448 | tf_op jit(solution)/shard_map/reduce_scatter | solution.py:22
  687.3 0.9 copy-start.2
  687.3 1.7 copy-start.4
Sparse Core Ops, SparseCore 0:
  9.7 27.5 all-gather.24
  79.0 103.9 all-reduce.2
  185.3 24.7 all-gather.14
  217.4 45.5 all-gather.16
  270.2 84.0 all-gather.26
  356.0 25.7 all-gather.12
  394.3 78.0 reduce-scatter.2
  474.3 24.3 all-gather.20
  516.3 45.5 all-gather.22
  567.0 84.0 all-gather.28
  653.0 25.7 all-gather.18
  687.4 78.1 reduce-scatter.4
